TPU v7x, 32 devices: a whole 2x2x4 slice. The times are simulated.
32 devices in a mesh: seq: 16 (over z, x, core), head: 2 (over y).
Axes of the slice: x: 2, y: 2, z: 4, core: 2. Of those that a mesh axis runs over, the one named last changes fastest.
Arguments:
- step_tokens: bfloat16 [2, 12, 8, 2560], P(None, None, None, 'head'), may hold values from -6 to 6
- parents: int32 [2, 12, 8], replicated, may hold values from 0 to 7
- tail_cache: bfloat16 [12, 8, 64, 2048], P(None, 'head', 'seq'), may hold values from -192 to 192
- tail_len: int32 [12], replicated, may hold values from 0 to 62, as said below
- cache: bfloat16 [8, 2048, 2048], P(None, ('seq', 'head')), may hold values from -192 to 192
- cache_len: int32 [8], replicated, may hold values from 256 to 2048, as said below
- prompt_states: bfloat16 [4, 128, 2560], P(None, 'seq', 'head'), may hold values from -6 to 6
- prompt_len: int32 [4], replicated, may hold values from 32 to 128, as said below
- in_gain: float32 [2560], P('head'), may hold values from 0.5 to 1.5
- w_query: bfloat16 [2560, 2048], P('head', 'seq'), may hold values from -0.125 to 0.125
- w_keyval: bfloat16 [2560, 2048], P('head', 'seq'), may hold values from -0.125 to 0.125
- q_gain: float32 [256], replicated, may hold values from 0.6 to 32
- k_gain: float32 [256], replicated, may hold values from 0.6 to 32
- w_out: bfloat16 [2048, 2560], P('seq', 'head'), may hold values from -0.125 to 0.125
- post_gain: float32 [2560], P('head'), may hold values from 0.5 to 1.5
- ffn_gain: float32 [2560], P('head'), may hold values from 0.5 to 1.5
- w_gate: bfloat16 [2560, 10240], P('head', 'seq'), may hold values from -0.125 to 0.125
- w_up: bfloat16 [2560, 10240], P('head', 'seq'), may hold values from -0.125 to 0.125
- w_down: bfloat16 [10240, 2560], P('seq', 'head'), may hold values from -0.0625 to 0.0625
- final_gain: float32 [2560], P('head'), may hold values from 0.5 to 1.5
Outputs:
- decoded: bfloat16 [2, 12, 8, 2560], P(None, None, None, 'head')
Inputs may be any that keep to these rules, and one draw needn't show every extreme that they name: `tail_len`: the first 4 groups have 0; the largest entry is exactly 62. `cache_len`: the largest entry is exactly 2048. `prompt_len`: the largest entry is exactly 128.
All inputs are finite; a program needn't handle non-finite values.
Results may differ from a plain program's by a relative error of at most 0.0055.
The roundings to bfloat16 on the way count: a program that leaves them out, or rounds other values in their place, can miss the bound.
Values may be sent and summed in bfloat16 or wider, within the bound.
No kernel may reach another device: no remote copies, remote signals or barrier semaphores. Data moves between devices by JAX's collectives and lax.ppermute only.
A program may use at most 128 MiB of HBM per device.

v0:
```python
import jax
import jax.numpy as jnp
from jax import lax
from jax.sharding import PartitionSpec as P

D = 2560
QH = 8
KVH = 4
HD = 256
QD = 2048
EPS = 1e-06
NEG = -1e30
QSCALE = 0.0625


def norm_heads(values, gain, scale):
    shaped = values.reshape(values.shape[:-1] + (-1, gain.shape[0]))
    shaped = shaped * lax.rsqrt(jnp.mean(shaped * shaped, -1, keepdims=True) + EPS) * gain * scale
    return shaped.reshape(values.shape)


def finish_keys(pairs, k_gain):
    half = pairs.shape[-1] // 2
    keys = norm_heads(pairs[..., :half], k_gain, 1.0)
    return jnp.concatenate([keys, pairs[..., half:]], -1).astype(jnp.bfloat16)


def split_pairs(pairs):
    half = pairs.shape[-1] // 2
    keys = pairs[..., :half].reshape(pairs.shape[:-1] + (KVH, HD))
    values = pairs[..., half:].reshape(pairs.shape[:-1] + (KVH, HD))
    return (keys, values)


def project_tokens(tokens, in_gain, w_query, w_keyval, q_gain, k_gain):
    flat = tokens.reshape(-1, tokens.shape[-1]).astype(jnp.float32)
    scaled = (flat * in_gain).astype(jnp.bfloat16)
    q_part = jnp.dot(scaled, w_query, preferred_element_type=jnp.float32)
    kv_part = jnp.dot(scaled, w_keyval, preferred_element_type=jnp.float32)
    squares = jnp.sum(flat * flat, -1)
    q_part, kv_part, squares = lax.psum((q_part, kv_part, squares), "head")
    factor = lax.rsqrt(squares / D + EPS)[:, None]
    q_raw = (q_part * factor).astype(jnp.bfloat16)
    kv_raw = (kv_part * factor).astype(jnp.bfloat16)
    q_raw, kv_raw = (
        lax.all_gather(q_raw, "seq", axis=1, tiled=True),
        lax.all_gather(kv_raw, "seq", axis=1, tiled=True),
    )
    queries = norm_heads(q_raw.astype(jnp.float32), q_gain, QSCALE).astype(jnp.bfloat16)
    fresh = finish_keys(kv_raw.astype(jnp.float32), k_gain)
    return (queries, fresh)


def shards(
    step_tokens,
    parents,
    tail_cache,
    tail_len,
    cache,
    cache_len,
    prompt_states,
    prompt_len,
    in_gain,
    w_query,
    w_keyval,
    q_gain,
    k_gain,
    w_out,
    post_gain,
    ffn_gain,
    w_gate,
    w_up,
    w_down,
    final_gain,
):
    f32 = jnp.float32
    bf16 = jnp.bfloat16
    n_head = lax.axis_size("head")
    n_seq = lax.axis_size("seq")
    seq_at = lax.axis_index("seq")
    head_at = lax.axis_index("head")
    flat_at = seq_at * n_head + head_at
    steps, groups, beams, width = step_tokens.shape
    pre = prompt_states.shape[0]
    repeat = QH // KVH
    col_block = QD // n_seq
    block_head = jnp.arange(n_seq) * col_block // HD
    head_pick = (jnp.arange(QH)[:, None] == block_head[None, :]).astype(f32)
    rows = jnp.transpose(prompt_states, (1, 0, 2)).astype(f32)
    prompt_scaled = (rows * in_gain).astype(bf16).reshape(-1, width)
    prompt_squares = jnp.sum(rows * rows, -1).reshape(-1)
    prompt_terms = jnp.dot(
        prompt_scaled,
        lax.all_gather(w_keyval, "seq", axis=1, tiled=True),
        preferred_element_type=f32,
    )
    prompt_sum, prompt_sq = (
        lax.psum_scatter(prompt_terms, "head", scatter_dimension=0, tiled=True),
        lax.psum_scatter(prompt_squares, "head", scatter_dimension=0, tiled=True),
    )
    prompt_pairs = finish_keys(prompt_sum * lax.rsqrt(prompt_sq / D + EPS)[:, None], k_gain)
    prompt_seg = prompt_pairs.shape[0] // pre
    prompt_pairs = jnp.transpose(prompt_pairs.reshape(prompt_seg, pre, -1), (1, 0, 2))
    prompt_keys, prompt_values = split_pairs(prompt_pairs)
    prompt_ok = (flat_at * prompt_seg + jnp.arange(prompt_seg))[None, :] < prompt_len[:, None]
    cache_seg = cache.shape[1]
    cache_keys, cache_values = split_pairs(cache)
    cache_ok = (flat_at * cache_seg + jnp.arange(cache_seg))[None, :] < cache_len[:, None]
    tail_seg = tail_cache.shape[2]
    local_beams = tail_cache.shape[1]
    beam_ids = head_at * local_beams + jnp.arange(local_beams)
    offset = (seq_at * tail_seg + jnp.arange(tail_seg))[None, :] - tail_len[:, None]
    all_beams = jnp.arange(beams)
    every_query, every_fresh = project_tokens(
        step_tokens, in_gain, w_query, w_keyval, q_gain, k_gain
    )
    every_query = every_query.reshape(steps, groups, beams, -1)
    every_fresh = every_fresh.reshape(steps, groups, beams, -1)
    tail_state = tail_cache
    decoded = []
    for step in range(steps):
        query = every_query[step]
        new_pairs = every_fresh[step]
        everyone = lax.all_gather(tail_state, "head", axis=1, tiled=True)
        picks = lax.dynamic_slice_in_dim(parents[step], head_at * local_beams, local_beams, 1)
        tail_state = jnp.take_along_axis(everyone, picks[:, :, None, None], axis=1)
        owner = jnp.broadcast_to(all_beams[None, :, None], (groups, beams, tail_seg))
        mine = lax.dynamic_slice_in_dim(new_pairs, head_at * local_beams, local_beams, 1)
        tail_state = jnp.where((offset == step)[:, None, :, None], mine[:, :, None, :], tail_state)
        tail_ok = (offset <= step)[:, None, None, :] & (
            owner[:, :, None, :] == beam_ids[None, None, :, None]
        )
        shaped = query.reshape(groups, beams, KVH, repeat, HD)
        tail_keys, tail_values = split_pairs(tail_state)
        pre_scores = jnp.einsum(
            "gbkrd,gtkd->gbkrt", shaped[:pre], prompt_keys, preferred_element_type=f32
        )
        dec_scores = jnp.einsum(
            "gbkrd,gtkd->gbkrt", shaped[pre:], cache_keys, preferred_element_type=f32
        )
        tail_scores = jnp.einsum(
            "gbkrd,gctkd->gbkrct", shaped, tail_keys, preferred_element_type=f32
        )
        pre_mask = prompt_ok[:, None, None, None, :]
        dec_mask = cache_ok[:, None, None, None, :]
        tail_mask = tail_ok[:, :, None, None, :, :]
        pre_scores = jnp.where(pre_mask, pre_scores, NEG)
        dec_scores = jnp.where(dec_mask, dec_scores, NEG)
        tail_scores = jnp.where(tail_mask, tail_scores, NEG)
        top = jnp.concatenate([jnp.max(pre_scores, -1), jnp.max(dec_scores, -1)], 0)
        top = jnp.maximum(top, jnp.max(tail_scores, (-2, -1)))
        top = lax.pmax(top, ("seq", "head"))
        pre_weights = jnp.where(pre_mask, jnp.exp(pre_scores - top[:pre, ..., None]), 0.0)
        dec_weights = jnp.where(dec_mask, jnp.exp(dec_scores - top[pre:, ..., None]), 0.0)
        tail_weights = jnp.where(tail_mask, jnp.exp(tail_scores - top[..., None, None]), 0.0)
        total = jnp.concatenate([jnp.sum(pre_weights, -1), jnp.sum(dec_weights, -1)], 0)
        total = total + jnp.sum(tail_weights, (-2, -1))
        weighted = jnp.concatenate(
            [
                jnp.einsum(
                    "gbkrt,gtkd->gbkrd",
                    pre_weights.astype(bf16),
                    prompt_values,
                    preferred_element_type=f32,
                ),
                jnp.einsum(
                    "gbkrt,gtkd->gbkrd",
                    dec_weights.astype(bf16),
                    cache_values,
                    preferred_element_type=f32,
                ),
            ],
            0,
        )
        weighted = weighted + jnp.einsum(
            "gbkrct,gctkd->gbkrd",
            tail_weights.astype(bf16),
            tail_values,
            preferred_element_type=f32,
        )
        weighted = weighted.reshape(groups * beams, -1)
        total = total.reshape(groups * beams, -1)
        spread_total = jnp.sum(total[:, :, None] * head_pick[None, :, :], 1)
        share, own_total = (
            lax.psum_scatter(weighted, "seq", scatter_dimension=1, tiled=True),
            lax.psum_scatter(spread_total, "seq", scatter_dimension=1, tiled=True),
        )
        share, own_total = lax.psum((share, own_total), "head")
        attn = (share / own_total).astype(bf16)
        partial_out = jnp.dot(attn, w_out, preferred_element_type=f32)
        out_proj = lax.psum(partial_out, "seq")
        out_sq = lax.psum(jnp.sum(out_proj * out_proj, -1), "head")
        x_f = step_tokens[step].reshape(groups * beams, -1).astype(f32)
        state = (x_f + out_proj * lax.rsqrt(out_sq / D + EPS)[:, None] * post_gain).astype(bf16)
        state = lax.optimization_barrier(state)
        state_f = state.astype(f32)
        scaled_two = (state_f * ffn_gain).astype(bf16)
        gate_part = jnp.dot(scaled_two, w_gate, preferred_element_type=f32)
        up_part = jnp.dot(scaled_two, w_up, preferred_element_type=f32)
        gate_part, up_part, state_sq = lax.psum(
            (gate_part, up_part, jnp.sum(state_f * state_f, -1)), "head"
        )
        norm_s = lax.rsqrt(state_sq / D + EPS)[:, None]
        inner = (jax.nn.gelu(gate_part * norm_s, approximate=True) * (up_part * norm_s)).astype(
            bf16
        )
        ffn_out = lax.psum(jnp.dot(inner, w_down, preferred_element_type=f32), "seq")
        ffn_sq = lax.psum(jnp.sum(ffn_out * ffn_out, -1), "head")
        result = (state_f + ffn_out * lax.rsqrt(ffn_sq / D + EPS)[:, None] * final_gain).astype(
            bf16
        )
        decoded.append(result.reshape(groups, beams, -1))
    return jnp.stack(decoded)


def solution(mesh):
    return jax.shard_map(
        shards,
        mesh=mesh,
        in_specs=(
            P(None, None, None, "head"),
            P(),
            P(None, "head", "seq", None),
            P(),
            P(None, ("seq", "head"), None),
            P(),
            P(None, "seq", "head"),
            P(),
            P("head"),
            P("head", "seq"),
            P("head", "seq"),
            P(),
            P(),
            P("seq", "head"),
            P("head"),
            P("head"),
            P("head", "seq"),
            P("head", "seq"),
            P("seq", "head"),
            P("head"),
        ),
        out_specs=P(None, None, None, "head"),
        check_vma=False,
    )
```

profile of v0, /device:TPU:0, one launch (start us, length us, event | category | flops | bytes accessed | tf_op | source)
XLA Modules:
  0.0 628.8 jit_solution(9408125753058318404)
XLA Ops:
  12.6 5.8 all-reduce.11
  19.1 17.0 %all-reduce.28.cloned.1.call-done = (f32[192,128]{1,0:T(8,128)}, f32[192,128]{1,0:T(8,128)}) async-done(((f32[192,128]{1,0:T(8,128)}, f32[192,128]{1,0:T(8,128)}), (f32[192,128]{1,0:T(8,128)}, f32[192,128]{1,0:T(8,128)})) %all-reduce.28.cloned.1.call-update) | async-done | bytes 196624 | tf_op jit(solution)/shard_map/psum | solution.py:41
  37.1 23.5 %all_gather.17 = bf16[192,2048]{1,0:T(8,128)(2,1)S(1)} all-gather(bf16[192,128]{1,0:T(8,128)(2,1)S(1)} %get-tuple-element.70), channel_id=1, replica_groups=mesh['seq'=16,'head'=2] {'seq'}, dimensions={1}, use_global_device_ids=true | all-gather | bytes 835584 | tf_op jit(solution)/shard_map/all_gather | solution.py:47
  66.4 2.9 gather_fusion
  73.5 2.7 fusion.131
  83.1 22.2 %all_gather.16 = bf16[192,2048]{1,0:T(8,128)(2,1)S(1)} all-gather(bf16[192,128]{1,0:T(8,128)(2,1)S(1)} %get-tuple-element.71), channel_id=1, replica_groups=mesh['seq'=16,'head'=2] {'seq'}, dimensions={1}, use_global_device_ids=true | all-gather | bytes 835584 | tf_op jit(solution)/shard_map/all_gather | solution.py:46
  107.2 2.4 reduce_sum.180
  121.2 2.0 fusion.37
  124.3 4.0 gather_fusion.1
  130.2 28.0 %all-gather.4.cloned.1.call-done = bf16[1280,2048]{1,0:T(8,128)(2,1)} async-done(((bf16[1280,128]{1,0:T(8,128)(2,1)}), bf16[1280,2048]{1,0:T(8,128)(2,1)}) %all-gather.4.cloned.1.call-update) | async-done | bytes 5242896 | tf_op jit(solution)/shard_map/all_gather | solution.py:94
  158.2 4.2 fusion.143
  164.5 2.1 fusion.34
  167.7 4.7 reduce-scatter.4.cloned.1.call-done
  177.9 40.8 %all-reduce.3 = (f32[12,8,4,2]{1,3,2,0:T(2,128)S(1)}, f32[12,8,4,2]{1,3,2,0:T(2,128)S(1)}) all-reduce(f32[12,8,4,2]{1,3,2,0:T(2,128)S(1)} %maximum_maximum_fusion.1, f32[12,8,4,2]{1,3,2,0:T(2,128)S(1)} %maximum_maximum_fusion), channel_id=1, replica_groups=mesh['seq'=16,'head'=2] {'seq','head'}, use_global_device_ids=true, to_apply=%region_35.37 | all-reduce | flops 1536 | bytes 12288 | tf_op jit(solution)/shard_map/pmax | solution.py:152
  235.1 60.1 %all-reduce.4 = (f32[96,16]{0,1:T(8,128)S(1)}, f32[96,16]{0,1:T(8,128)S(1)}) all-reduce(f32[96,16]{0,1:T(8,128)S(1)} %get-tuple-element.7, f32[96,16]{0,1:T(8,128)S(1)} %get-tuple-element.6), channel_id=7, replica_groups=mesh['seq'=16,'head'=2] {'seq'}, use_global_device_ids=true, to_apply=%region_42.44.clone | all-reduce | flops 3072 | bytes 24576
  297.6 45.9 %reduce-scatter.8.cloned.1.call-done = f32[96,128]{1,0:T(8,128)} async-done(((f32[96,2048]{1,0:T(8,128)}), f32[96,128]{1,0:T(8,128)}) %reduce-scatter.8.cloned.1.call-update) | async-done | bytes 49168 | tf_op jit(solution)/shard_map/reduce_scatter | solution.py:185
  343.6 22.5 %all-reduce.24.cloned.1.call-done = (f32[96,128]{1,0:T(8,128)}, f32[96]{0:T(128)}, f32[96,128]{1,0:T(8,128)}, f32[96]{0:T(128)}) async-done(((f32[96,128]{1,0:T(8,128)}, f32[96]{0:T(128)}, f32[96,128]{1,0:T(8,128)}, f32[96]{0:T(128)}), (f32[96,128]{1,0:T(8,128)}, f32[96]{0:T(128)}, f32[96,128]{1,0:T(8,128)}, f32[96]{0:T(128)})) %all-reduce.24.cloned.1.call-update) | async-done | bytes 99088 | tf_op jit(solution)/shard_map/psum | solution.py:188
  369.9 94.0 %all-reduce.22.cloned.1.call-done = (f32[96,1280]{1,0:T(8,128)}, f32[96,1280]{1,0:T(8,128)}) async-done(((f32[96,1280]{1,0:T(8,128)}, f32[96,1280]{1,0:T(8,128)}), (f32[96,1280]{1,0:T(8,128)}, f32[96,1280]{1,0:T(8,128)})) %all-reduce.22.cloned.1.call-update) | async-done | bytes 983056 | tf_op jit(solution)/shard_map/psum | solution.py:191
  466.2 4.9 all-reduce.9
  477.7 4.9 all-reduce.8
  482.7 33.1 %all-reduce.26.cloned.1.call-done = (f32[96,640]{1,0:T(8,128)}, f32[96,640]{1,0:T(8,128)}, f32[96,640]{1,0:T(8,128)}, f32[96,640]{1,0:T(8,128)}) async-done(((f32[96,640]{1,0:T(8,128)}, f32[96,640]{1,0:T(8,128)}, f32[96,640]{1,0:T(8,128)}, f32[96,640]{1,0:T(8,128)}), (f32[96,640]{1,0:T(8,128)}, f32[96,640]{1,0:T(8,128)}, f32[96,640]{1,0:T(8,128)}, f32[96,640]{1,0:T(8,128)})) %all-reduce.26.cloned.1.call-update) | async-done | bytes 983056 | tf_op jit(solution)/shard_map/psum | solution.py:200
  515.7 2.4 fusion.81
  519.5 93.3 %all-reduce.20.cloned.1.call-done = (f32[96,1280]{1,0:T(8,128)}, f32[96,1280]{1,0:T(8,128)}) async-done(((f32[96,1280]{1,0:T(8,128)}, f32[96,1280]{1,0:T(8,128)}), (f32[96,1280]{1,0:T(8,128)}, f32[96,1280]{1,0:T(8,128)})) %all-reduce.20.cloned.1.call-update) | async-done | bytes 983056 | tf_op jit(solution)/shard_map/psum | solution.py:207
  615.1 4.9 all-reduce.7
  (282 shorter events, 85.6 us)
Async XLA Ops:
  6.5 509.2 %copy-start = (bf16[640,1280]{1,0:T(8,128)(2,1)S(1)}, bf16[640,1280]{1,0:T(8,128)(2,1)}, u32[]{:S(2)}) copy-start(bf16[640,1280]{1,0:T(8,128)(2,1)} %param.40) | copy-start | bytes 4915204
  6.5 29.6 %all-reduce.28.cloned.1.call-start = ((), (), s32[]{:S(2)}) async-start(), calls=%async_computation.13 | async-start | bytes 393216 | tf_op jit(solution)/shard_map/psum | solution.py:41
  7.9 10.6 %copy-start.47 = (s32[12]{0:T(128)S(1)}, s32[12]{0:T(128)}, u32[]{:S(2)}) copy-start(s32[12]{0:T(128)} %param.25) | copy-start | bytes 148
  10.8 55.7 %all-gather.6.cloned.1.call-start = ((), (), s32[]{:S(2)}) async-start(), calls=%async_computation.5 | async-start | bytes 2359296 | tf_op jit(solution)/shard_map/all_gather | solution.py:124
  11.5 112.7 %all-gather.8.cloned.1.call-start = ((), (), s32[]{:S(2)}) async-start(), calls=%async_computation.7 | async-start | bytes 2359296 | tf_op jit(solution)/shard_map/all_gather | solution.py:124
  11.8 52.8 %copy-start.32 = (f32[1,2,4,128]{3,1,2,0:T(2,128)}, f32[1,2,4,128]{3,1,2,0:T(2,128)S(1)}, u32[]{:S(2)}) copy-start(f32[1,2,4,128]{3,1,2,0:T(2,128)S(1)} %copy.245) | copy-start | bytes 12292
  71.1 87.1 %all-gather.4.cloned.1.call-start = ((), (), s32[]{:S(2)}) async-start(), calls=%async_computation.3 | async-start | bytes 5570560 | tf_op jit(solution)/shard_map/all_gather | solution.py:94
  71.6 100.7 %reduce-scatter.4.cloned.1.call-start = ((), (), s32[]{:S(2)}) async-start(), calls=%async_computation.4 | async-start | bytes 393216 | tf_op jit(solution)/shard_map/reduce_scatter | solution.py:98
  82.4 33.9 %copy-start.35 = (pred[8,64]{1,0:T(8,128)(4,1)}, pred[8,64]{1,0:T(8,128)(4,1)S(1)}, u32[]{:S(2)}) copy-start(pred[8,64]{1,0:T(8,128)(4,1)S(1)} %broadcast_compare_fusion) | copy-start | bytes 1540
  83.1 41.0 %copy-start.24 = (pred[12,8,4,4]{0,1,3,2:T(8,128)(4,1)}, pred[12,8,4,4]{0,1,3,2:T(8,128)(4,1)S(1)}, u32[]{:S(2)}) copy-start(pred[12,8,4,4]{0,1,3,2:T(8,128)(4,1)S(1)} %get-tuple-element.72) | copy-start | bytes 4612
  124.3 33.9 %copy-start.17 = (bf16[32,1280]{1,0:T(8,128)(2,1)S(1)}, bf16[32,1280]{1,0:T(8,128)(2,1)}, u32[]{:S(2)}) copy-start(bf16[32,1280]{1,0:T(8,128)(2,1)} %reshape.371) | copy-start | bytes 245764
  162.4 135.2 %reduce-scatter.6.cloned.1.call-start = ((), (), s32[]{:S(2)}) async-start(), calls=%async_computation.6 | async-start | bytes 835584 | tf_op jit(solution)/shard_map/reduce_scatter | solution.py:185
  167.5 10.4 %copy-start.28 = (f32[8,8,4,2]{1,3,2,0:T(2,128)S(1)}, f32[8,8,4,2]{1,3,2,0:T(2,128)}, u32[]{:S(2)}) copy-start(f32[8,8,4,2]{1,3,2,0:T(2,128)} %get-tuple-element.74) | copy-start | bytes 6148
  173.8 50.0 %copy-start.12 = (f32[8,8,4,2,64]{4,1,3,2,0:T(8,128)S(1)}, f32[8,8,4,2,64]{4,1,3,2,0:T(8,128)}, u32[]{:S(2)}) copy-start(f32[8,8,4,2,64]{4,1,3,2,0:T(8,128)} %get-tuple-element.79) | copy-start | bytes 393220
  226.8 116.6 %reduce-scatter.8.cloned.1.call-start = ((), (), s32[]{:S(2)}) async-start(), calls=%async_computation.8 | async-start | bytes 835584 | tf_op jit(solution)/shard_map/reduce_scatter | solution.py:185
  233.1 133.0 %copy-start.10 = (bf16[128,1280]{1,0:T(8,128)(2,1)S(1)}, bf16[128,1280]{1,0:T(8,128)(2,1)}, u32[]{:S(2)}) copy-start(bf16[128,1280]{1,0:T(8,128)(2,1)} %param.35) | copy-start | bytes 983044
  233.1 133.0 %all-reduce.24.cloned.1.call-start = ((), (), s32[]{:S(2)}) async-start(), calls=%async_computation.11 | async-start | bytes 198656 | tf_op jit(solution)/shard_map/psum | solution.py:188
  343.5 120.4 %all-reduce.22.cloned.1.call-start = ((), (), s32[]{:S(2)}) async-start(), calls=%async_computation.10 | async-start | bytes 1966080 | tf_op jit(solution)/shard_map/psum | solution.py:191
  367.9 103.3 %copy-start.37 = (f32[1280]{0:T(1024)S(1)}, f32[1280]{0:T(1024)}, u32[]{:S(2)}) copy-start(f32[1280]{0:T(1024)} %param.36) | copy-start | bytes 15364
  369.8 103.1 %copy-start.2 = (bf16[1280,640]{1,0:T(8,128)(2,1)S(1)}, bf16[1280,640]{1,0:T(8,128)(2,1)}, u32[]{:S(2)}) copy-start(bf16[1280,640]{1,0:T(8,128)(2,1)} %param.39) | copy-start | bytes 4915204
  369.8 103.1 %copy-start.26 = (f32[1280]{0:T(1024)S(1)}, f32[1280]{0:T(1024)}, u32[]{:S(2)}) copy-start(f32[1280]{0:T(1024)} %param.37) | copy-start | bytes 15364
  369.9 145.9 %all-reduce.26.cloned.1.call-start = ((), (), s32[]{:S(2)}) async-start(), calls=%async_computation.12 | async-start | bytes 1966080 | tf_op jit(solution)/shard_map/psum | solution.py:200
  477.4 135.4 %all-reduce.20.cloned.1.call-start = ((), (), s32[]{:S(2)}) async-start(), calls=%async_computation.9 | async-start | bytes 1966080 | tf_op jit(solution)/shard_map/psum | solution.py:207
  519.4 100.6 %copy-start.38 = (f32[1280]{0:T(1024)S(1)}, f32[1280]{0:T(1024)}, u32[]{:S(2)}) copy-start(f32[1280]{0:T(1024)} %param.41) | copy-start | bytes 15364
  (40 other events, 141.6 us)
Sparse Core Ops, SparseCore 0:
  10.9 25.1 all-reduce.27
  37.6 27.1 all-gather.5
  71.2 25.6 all-gather.7
  98.9 59.2 all-gather.3
  162.5 9.8 reduce-scatter.3
  227.0 57.3 reduce-scatter.5
  287.9 55.5 reduce-scatter.7
  346.1 19.9 all-reduce.23
  370.0 93.8 all-reduce.21
  477.5 38.1 all-reduce.25
  519.6 93.1 all-reduce.19
where the time goes:
time: 630 us; the launch traced here: 629 us
  waiting for transfers between devices  340 us (54%)
  blocking collectives  167 us (27%)
  local copies, waits for them, and re-layouts  40.9 us (6%)
  matrix products  38.3 us (6%)
  other arithmetic  27.2 us (4%)
  between operations  14.9 us (2%)
    psum x1, waiting for transfers between devices, shards(): out_proj = lax.psum(partial_out, 'seq')  94 us
    psum x1, waiting for transfers between devices, shards(): lax.psum(jnp.dot(inner, w_down, preferred_element_type=f32), 'seq')  93.3 us
    unnamed x1, blocking collectives  60.1 us
    reduce_scatter x2, waiting for transfers between devices, shards(): lax.psum_scatter(weighted, 'seq', scatter_dimension=1, tiled=True)  45.9 us
    pmax x1, blocking collectives, shards(): top = lax.pmax(top, ('seq', 'head'))  40.8 us
    psum x1, waiting for transfers between devices, shards(): lax.psum((gate_part, up_part, jnp.sum(state_f * state_f, -1)), 'head')  33.1 us
    all_gather x1, waiting for transfers between devices, shards(): lax.all_gather(w_keyval, 'seq', axis=1, tiled=True)  28 us
    all_gather x1, blocking collectives, project_tokens(): lax.all_gather(kv_raw, 'seq', axis=1, tiled=True)  23.5 us
  transfers between devices with their start and end apart: 11, of which 8 were waited for; matrix products, arithmetic and copies ran while one was open for 9% of the time, Pallas kernels for 0%

commit v1 on v0

--- a/solution.py
+++ b/solution.py
@@ -11,6 +11,27 @@
 EPS = 1e-06
 NEG = -1e30
 QSCALE = 0.0625
+
+
+def laid_out(pieces, dim):
+    shape = list(pieces.shape[1:])
+    shape[dim] *= pieces.shape[0]
+    return jnp.moveaxis(pieces, 0, dim).reshape(shape)
+
+
+def doubled(x, axis):
+    devices, position = (lax.axis_size(axis), lax.axis_index(axis))
+    parts, distance = (x[None], 1)
+    while distance < devices:
+        other = lax.ppermute(parts, axis, [(i, i ^ distance) for i in range(devices)])
+        low = position & distance == 0
+        parts = jnp.concatenate([jnp.where(low, parts, other), jnp.where(low, other, parts)])
+        distance *= 2
+    return parts
+
+
+def doubled_up(shard, axis, dim):
+    return laid_out(doubled(shard, axis), dim)
 
 
 def norm_heads(values, gain, scale):
@@ -42,10 +63,7 @@
     factor = lax.rsqrt(squares / D + EPS)[:, None]
     q_raw = (q_part * factor).astype(jnp.bfloat16)
     kv_raw = (kv_part * factor).astype(jnp.bfloat16)
-    q_raw, kv_raw = (
-        lax.all_gather(q_raw, "seq", axis=1, tiled=True),
-        lax.all_gather(kv_raw, "seq", axis=1, tiled=True),
-    )
+    q_raw, kv_raw = (doubled_up(q_raw, "seq", 1), lax.all_gather(kv_raw, "seq", axis=1, tiled=True))
     queries = norm_heads(q_raw.astype(jnp.float32), q_gain, QSCALE).astype(jnp.bfloat16)
     fresh = finish_keys(kv_raw.astype(jnp.float32), k_gain)
     return (queries, fresh)

time: 630 us -> 630 us (level)
  blocking collectives: 167 us -> 145 us
  waiting for transfers between devices: 340 us -> 361 us
    all_gather x1 -> x0, blocking collectives: 22.2 us -> none  [project_tokens(): lax.all_gather(q_raw, 'seq', axis=1, tiled=True)]
    ppermute x0 -> x4, waiting for transfers between devices: none -> 18 us  [doubled(): lax.ppermute(parts, axis, [(i, i ^ distance) for i in range(devices)])]
  transfers between devices with their start and end apart: 11 -> 15, of which waited for: 8 -> 12; matrix products, arithmetic and copies ran while one was open for 9% -> 9% of each run, Pallas kernels for 0% -> 0%
where the time goes in v1:
time: 630 us; the launch traced here: 629 us
  waiting for transfers between devices  361 us (57%)
  blocking collectives  145 us (23%)
  local copies, waits for them, and re-layouts  40.8 us (6%)
  matrix products  38.1 us (6%)
  other arithmetic  25.6 us (4%)
  between operations  15 us (2%)
    psum x1, waiting for transfers between devices, shards(): out_proj = lax.psum(partial_out, 'seq')  94 us
    psum x1, waiting for transfers between devices, shards(): lax.psum(jnp.dot(inner, w_down, preferred_element_type=f32), 'seq')  93.3 us
    unnamed x1, blocking collectives  60 us
    reduce_scatter x2, waiting for transfers between devices, shards(): lax.psum_scatter(weighted, 'seq', scatter_dimension=1, tiled=True)  46 us
    pmax x1, blocking collectives, shards(): top = lax.pmax(top, ('seq', 'head'))  40.8 us
    psum x1, waiting for transfers between devices, shards(): lax.psum((gate_part, up_part, jnp.sum(state_f * state_f, -1)), 'head')  33.1 us
    all_gather x1, waiting for transfers between devices, shards(): lax.all_gather(w_keyval, 'seq', axis=1, tiled=True)  31.3 us
    all_gather x1, blocking collectives, project_tokens(): lax.all_gather(kv_raw, 'seq', axis=1, tiled=True)  23.5 us
  transfers between devices with their start and end apart: 15, of which 12 were waited for; matrix products, arithmetic and copies ran while one was open for 9% of the time, Pallas kernels for 0%

profile of v1, /device:TPU:0, one launch (start us, length us, event | category | flops | bytes accessed | tf_op | source)
XLA Modules:
  0.0 628.7 jit_solution(13528066797220769758)
XLA Ops:
  13.1 5.8 all-reduce.11
  19.6 16.5 %all-reduce.28.cloned.1.call-done = (f32[192,128]{1,0:T(8,128)}, f32[192,128]{1,0:T(8,128)}) async-done(((f32[192,128]{1,0:T(8,128)}, f32[192,128]{1,0:T(8,128)}), (f32[192,128]{1,0:T(8,128)}, f32[192,128]{1,0:T(8,128)})) %all-reduce.28.cloned.1.call-update) | async-done | bytes 196624 | tf_op jit(solution)/shard_map/psum | solution.py:62
  37.1 23.5 %all_gather.13 = bf16[192,2048]{1,0:T(8,128)(2,1)S(1)} all-gather(bf16[192,128]{1,0:T(8,128)(2,1)S(1)} %get-tuple-element.78), channel_id=1, replica_groups=mesh['seq'=16,'head'=2] {'seq'}, dimensions={1}, use_global_device_ids=true | all-gather | bytes 835584 | tf_op jit(solution)/shard_map/all_gather | solution.py:66
  65.7 2.9 gather_fusion
  71.5 2.8 fusion.133
  76.3 4.4 collective-permute-done.1
  81.8 5.3 collective-permute-done.2
  99.2 7.4 %collective-permute-done.3 = bf16[8,192,128]{2,1,0:T(8,128)(2,1)} collective-permute-done((bf16[8,192,128]{2,1,0:T(8,128)(2,1)S(1)}, bf16[8,192,128]{2,1,0:T(8,128)(2,1)}, u32[]{:S(2)}, u32[]{:S(2)}) %collective-permute-start.3) | collective-permute-done | bytes 393248 | tf_op jit(solution)/shard_map/ppermute | solution.py:26
  121.1 4.0 gather_fusion.1
  126.9 31.3 %all-gather.4.cloned.1.call-done = bf16[1280,2048]{1,0:T(8,128)(2,1)} async-done(((bf16[1280,128]{1,0:T(8,128)(2,1)}), bf16[1280,2048]{1,0:T(8,128)(2,1)}) %all-gather.4.cloned.1.call-update) | async-done | bytes 5242896 | tf_op jit(solution)/shard_map/all_gather | solution.py:112
  158.2 4.2 fusion.145
  164.6 2.1 fusion.35
  167.7 4.8 reduce-scatter.4.cloned.1.call-done
  178.0 40.8 %all-reduce.3 = (f32[12,8,4,2]{1,3,2,0:T(2,128)S(1)}, f32[12,8,4,2]{1,3,2,0:T(2,128)S(1)}) all-reduce(f32[12,8,4,2]{1,3,2,0:T(2,128)S(1)} %maximum_maximum_fusion.1, f32[12,8,4,2]{1,3,2,0:T(2,128)S(1)} %maximum_maximum_fusion), channel_id=1, replica_groups=mesh['seq'=16,'head'=2] {'seq','head'}, use_global_device_ids=true, to_apply=%region_36.38 | all-reduce | flops 1536 | bytes 12288 | tf_op jit(solution)/shard_map/pmax | solution.py:170
  235.1 60.0 %all-reduce.4 = (f32[96,16]{0,1:T(8,128)S(1)}, f32[96,16]{0,1:T(8,128)S(1)}) all-reduce(f32[96,16]{0,1:T(8,128)S(1)} %get-tuple-element.7, f32[96,16]{0,1:T(8,128)S(1)} %get-tuple-element.6), channel_id=7, replica_groups=mesh['seq'=16,'head'=2] {'seq'}, use_global_device_ids=true, to_apply=%region_43.45.clone | all-reduce | flops 3072 | bytes 24576
  297.4 46.0 %reduce-scatter.8.cloned.1.call-done = f32[96,128]{1,0:T(8,128)} async-done(((f32[96,2048]{1,0:T(8,128)}), f32[96,128]{1,0:T(8,128)}) %reduce-scatter.8.cloned.1.call-update) | async-done | bytes 49168 | tf_op jit(solution)/shard_map/reduce_scatter | solution.py:203
  343.5 22.5 %all-reduce.24.cloned.1.call-done = (f32[96,128]{1,0:T(8,128)}, f32[96]{0:T(128)}, f32[96,128]{1,0:T(8,128)}, f32[96]{0:T(128)}) async-done(((f32[96,128]{1,0:T(8,128)}, f32[96]{0:T(128)}, f32[96,128]{1,0:T(8,128)}, f32[96]{0:T(128)}), (f32[96,128]{1,0:T(8,128)}, f32[96]{0:T(128)}, f32[96,128]{1,0:T(8,128)}, f32[96]{0:T(128)})) %all-reduce.24.cloned.1.call-update) | async-done | bytes 99088 | tf_op jit(solution)/shard_map/psum | solution.py:206
  369.8 94.0 %all-reduce.22.cloned.1.call-done = (f32[96,1280]{1,0:T(8,128)}, f32[96,1280]{1,0:T(8,128)}) async-done(((f32[96,1280]{1,0:T(8,128)}, f32[96,1280]{1,0:T(8,128)}), (f32[96,1280]{1,0:T(8,128)}, f32[96,1280]{1,0:T(8,128)})) %all-reduce.22.cloned.1.call-update) | async-done | bytes 983056 | tf_op jit(solution)/shard_map/psum | solution.py:209
  466.1 4.9 all-reduce.9
  477.6 4.9 all-reduce.8
  482.6 33.1 %all-reduce.26.cloned.1.call-done = (f32[96,640]{1,0:T(8,128)}, f32[96,640]{1,0:T(8,128)}, f32[96,640]{1,0:T(8,128)}, f32[96,640]{1,0:T(8,128)}) async-done(((f32[96,640]{1,0:T(8,128)}, f32[96,640]{1,0:T(8,128)}, f32[96,640]{1,0:T(8,128)}, f32[96,640]{1,0:T(8,128)}), (f32[96,640]{1,0:T(8,128)}, f32[96,640]{1,0:T(8,128)}, f32[96,640]{1,0:T(8,128)}, f32[96,640]{1,0:T(8,128)})) %all-reduce.26.cloned.1.call-update) | async-done | bytes 983056 | tf_op jit(solution)/shard_map/psum | solution.py:218
  515.6 2.4 fusion.82
  519.4 93.3 %all-reduce.20.cloned.1.call-done = (f32[96,1280]{1,0:T(8,128)}, f32[96,1280]{1,0:T(8,128)}) async-done(((f32[96,1280]{1,0:T(8,128)}, f32[96,1280]{1,0:T(8,128)}), (f32[96,1280]{1,0:T(8,128)}, f32[96,1280]{1,0:T(8,128)})) %all-reduce.20.cloned.1.call-update) | async-done | bytes 983056 | tf_op jit(solution)/shard_map/psum | solution.py:225
  615.0 4.9 all-reduce.7
  (297 shorter events, 91.8 us)
Async XLA Ops:
  6.5 509.1 %copy-start = (bf16[640,1280]{1,0:T(8,128)(2,1)S(1)}, bf16[640,1280]{1,0:T(8,128)(2,1)}, u32[]{:S(2)}) copy-start(bf16[640,1280]{1,0:T(8,128)(2,1)} %param.40) | copy-start | bytes 4915204
  6.5 29.6 %all-reduce.28.cloned.1.call-start = ((), (), s32[]{:S(2)}) async-start(), calls=%async_computation.13 | async-start | bytes 393216 | tf_op jit(solution)/shard_map/psum | solution.py:62
  10.8 54.9 %all-gather.6.cloned.1.call-start = ((), (), s32[]{:S(2)}) async-start(), calls=%async_computation.5 | async-start | bytes 2359296 | tf_op jit(solution)/shard_map/all_gather | solution.py:142
  11.5 109.6 %all-gather.8.cloned.1.call-start = ((), (), s32[]{:S(2)}) async-start(), calls=%async_computation.7 | async-start | bytes 2359296 | tf_op jit(solution)/shard_map/all_gather | solution.py:142
  11.8 52.8 %copy-start.33 = (f32[1,2,4,128]{3,1,2,0:T(2,128)}, f32[1,2,4,128]{3,1,2,0:T(2,128)S(1)}, u32[]{:S(2)}) copy-start(f32[1,2,4,128]{3,1,2,0:T(2,128)S(1)} %copy.282) | copy-start | bytes 12292
  70.3 87.9 %all-gather.4.cloned.1.call-start = ((), (), s32[]{:S(2)}) async-start(), calls=%async_computation.3 | async-start | bytes 5570560 | tf_op jit(solution)/shard_map/all_gather | solution.py:112
  70.9 101.6 %reduce-scatter.4.cloned.1.call-start = ((), (), s32[]{:S(2)}) async-start(), calls=%async_computation.4 | async-start | bytes 393216 | tf_op jit(solution)/shard_map/reduce_scatter | solution.py:116
  71.5 96.0 %copy-start.23 = (pred[12,8,4,4]{0,1,3,2:T(8,128)(4,1)}, pred[12,8,4,4]{0,1,3,2:T(8,128)(4,1)S(1)}, u32[]{:S(2)}) copy-start(pred[12,8,4,4]{0,1,3,2:T(8,128)(4,1)S(1)} %get-tuple-element.81) | copy-start | bytes 4612
  74.3 1.2 collective-permute-start
  75.6 5.1 collective-permute-start.1
  80.7 6.4 %collective-permute-start.2 = (bf16[4,192,128]{2,1,0:T(8,128)(2,1)S(1)}, bf16[4,192,128]{2,1,0:T(8,128)(2,1)S(1)}, u32[]{:S(2)}, u32[]{:S(2)}) collective-permute-start(bf16[4,192,128]{2,1,0:T(8,128)(2,1)S(1)} %pad_maximum_fusion.4), channel_id=1, source_target_pairs={{0,8},{2,10},{4,12},{6,14},{8,0},{10,2},{12,4},{14,6},{16,24},{18,... | collective-permute-start | bytes 589832 | tf_op jit(solution)/shard_map/ppermute | solution.py:26
  87.9 18.8 %collective-permute-start.3 = (bf16[8,192,128]{2,1,0:T(8,128)(2,1)S(1)}, bf16[8,192,128]{2,1,0:T(8,128)(2,1)}, u32[]{:S(2)}, u32[]{:S(2)}) collective-permute-start(bf16[8,192,128]{2,1,0:T(8,128)(2,1)S(1)} %pad_maximum_fusion.3), channel_id=1, source_target_pairs={{0,16},{2,18},{4,20},{6,22},{8,24},{10,26},{12,28},{14,30},{16,0},... | collective-permute-start | bytes 1179656 | tf_op jit(solution)/shard_map/ppermute | solution.py:26
  162.5 134.9 %reduce-scatter.6.cloned.1.call-start = ((), (), s32[]{:S(2)}) async-start(), calls=%async_computation.6 | async-start | bytes 835584 | tf_op jit(solution)/shard_map/reduce_scatter | solution.py:203
  173.9 50.0 %copy-start.14 = (f32[8,8,4,2,64]{4,1,3,2,0:T(8,128)S(1)}, f32[8,8,4,2,64]{4,1,3,2,0:T(8,128)}, u32[]{:S(2)}) copy-start(f32[8,8,4,2,64]{4,1,3,2,0:T(8,128)} %get-tuple-element.87) | copy-start | bytes 393220
  226.9 116.5 %reduce-scatter.8.cloned.1.call-start = ((), (), s32[]{:S(2)}) async-start(), calls=%async_computation.8 | async-start | bytes 835584 | tf_op jit(solution)/shard_map/reduce_scatter | solution.py:203
  233.0 133.0 %copy-start.12 = (bf16[128,1280]{1,0:T(8,128)(2,1)S(1)}, bf16[128,1280]{1,0:T(8,128)(2,1)}, u32[]{:S(2)}) copy-start(bf16[128,1280]{1,0:T(8,128)(2,1)} %param.35) | copy-start | bytes 983044
  233.0 132.9 %all-reduce.24.cloned.1.call-start = ((), (), s32[]{:S(2)}) async-start(), calls=%async_computation.11 | async-start | bytes 198656 | tf_op jit(solution)/shard_map/psum | solution.py:206
  343.4 120.4 %all-reduce.22.cloned.1.call-start = ((), (), s32[]{:S(2)}) async-start(), calls=%async_computation.10 | async-start | bytes 1966080 | tf_op jit(solution)/shard_map/psum | solution.py:209
  367.8 103.3 %copy-start.38 = (f32[1280]{0:T(1024)S(1)}, f32[1280]{0:T(1024)}, u32[]{:S(2)}) copy-start(f32[1280]{0:T(1024)} %param.36) | copy-start | bytes 15364
  369.7 103.1 %copy-start.2 = (bf16[1280,640]{1,0:T(8,128)(2,1)S(1)}, bf16[1280,640]{1,0:T(8,128)(2,1)}, u32[]{:S(2)}) copy-start(bf16[1280,640]{1,0:T(8,128)(2,1)} %param.39) | copy-start | bytes 4915204
  369.7 103.1 %copy-start.27 = (f32[1280]{0:T(1024)S(1)}, f32[1280]{0:T(1024)}, u32[]{:S(2)}) copy-start(f32[1280]{0:T(1024)} %param.37) | copy-start | bytes 15364
  369.8 145.9 %all-reduce.26.cloned.1.call-start = ((), (), s32[]{:S(2)}) async-start(), calls=%async_computation.12 | async-start | bytes 1966080 | tf_op jit(solution)/shard_map/psum | solution.py:218
  477.3 135.4 %all-reduce.20.cloned.1.call-start = ((), (), s32[]{:S(2)}) async-start(), calls=%async_computation.9 | async-start | bytes 1966080 | tf_op jit(solution)/shard_map/psum | solution.py:225
  519.4 100.6 %copy-start.39 = (f32[1280]{0:T(1024)S(1)}, f32[1280]{0:T(1024)}, u32[]{:S(2)}) copy-start(f32[1280]{0:T(1024)} %param.41) | copy-start | bytes 15364
  (45 other events, 287.2 us)
Sparse Core Ops, SparseCore 0:
  10.9 25.1 all-reduce.27
  37.7 27.1 all-gather.5
  70.5 26.4 all-gather.7
  99.0 59.2 all-gather.3
  162.6 9.8 reduce-scatter.3
  227.0 57.3 reduce-scatter.5
  287.9 55.4 reduce-scatter.7
  346.0 19.9 all-reduce.23
  369.9 93.8 all-reduce.21
  477.4 38.1 all-reduce.25
  519.5 93.1 all-reduce.19
